TPU v7x, 128 devices: a whole 4x4x4 slice. The times are simulated.
128 devices in a mesh: pipe: 4 (over x_hi, core), dp: 16 (over y, z), tensor: 2 (over x_lo).
Axes of the slice: x: 4 (x_hi: 2, x_lo: 2; x = x_hi * 2 + x_lo), y: 4, z: 4, core: 2. Of those that a mesh axis runs over, the one named last changes fastest.
Arguments:
- hidden_states: bfloat16 [4, 4096, 8192], P('pipe', 'dp'), may hold values from -60 to 60
- norm_gain: bfloat16 [4, 8192], P('pipe'), may hold values from 0.5 to 2
- key_weight: bfloat16 [4, 8192, 512], P('pipe', 'dp', 'tensor'), may hold values from -0.0625 to 0.0625
- value_weight: bfloat16 [4, 8192, 512], P('pipe', 'dp', 'tensor'), may hold values from -0.0625 to 0.0625
- queries: bfloat16 [4, 4096, 4096], P('pipe', 'dp', 'tensor'), may hold values from -128 to 128
- context_cotangent: bfloat16 [4, 4096, 4096], P('pipe', 'dp', 'tensor'), may hold values from -96 to 96
- lengths: int32 [4, 16], P('pipe', 'dp'), may hold values from 64 to 256, as said below
- policy_logp: float32 [4, 16], P('pipe', 'dp'), may hold values from -90 to -30
- reference_logp: float32 [4, 16], P('pipe', 'dp'), may hold values from -90 to -30
Outputs:
- key_weight_grad: bfloat16 [4, 8192, 512], P('pipe', 'dp', 'tensor')
- value_weight_grad: bfloat16 [4, 8192, 512], P('pipe', 'dp', 'tensor')
- lower_cotangent: bfloat16 [4, 4096, 8192], P('pipe', 'dp')
Inputs may be any that keep to these rules, and one draw needn't show every extreme that they name: `lengths`: each sequence's live tokens; positions at or beyond it are padding.
All inputs are finite; a program needn't handle non-finite values.
Results may differ from a plain program's by a relative error of at most 0.015.
The roundings to bfloat16 on the way count: a program that leaves them out, or rounds other values in their place, can miss the bound.
Values may be sent and summed in bfloat16 or wider, within the bound.
No kernel may reach another device: no remote copies, remote signals or barrier semaphores. Data moves between devices by JAX's collectives and lax.ppermute only.
A program may use at most 128 MiB of HBM per device.

v0:
```python
import math
import jax
import jax.numpy as jnp
from jax import lax
from jax.sharding import PartitionSpec as P

HD = 128
npo_beta = 0.1
norm_eps = 1e-05
rope_base = 500000.0


def shifted(value, axis, steps):
    count = lax.axis_size(axis)
    leading, last = (max(0, -steps), min(count, count - steps))
    return lax.ppermute(value, axis, [(source, source + steps) for source in range(leading, last)])


def rope_tables(length, head_dim):
    positions = jnp.arange(length).astype(jnp.float32)
    freq_index = jnp.arange(head_dim // 2).astype(jnp.float32)
    inverse = 1.0 / rope_base ** (2.0 * freq_index / head_dim)
    angles = positions[:, None] * inverse[None, :]
    cosine = jnp.concatenate([jnp.cos(angles), jnp.cos(angles)], axis=1)
    sine = jnp.concatenate([jnp.sin(angles), jnp.sin(angles)], axis=1)
    return (cosine, sine)


def rotate_half(values):
    half = values.shape[-1] // 2
    return jnp.concatenate([-values[..., half:], values[..., :half]], axis=-1)


def rotate_back(values):
    half = values.shape[-1] // 2
    return jnp.concatenate([values[..., half:], -values[..., :half]], axis=-1)


def sequence_grads(query_seq, key_seq, value_seq, cotan_seq, length_seq, cosine, sine):
    seq_len, kv_heads, head_dim = key_seq.shape
    group = query_seq.shape[1] // kv_heads
    scale = 1.0 / math.sqrt(head_dim)
    query_g = query_seq.reshape(seq_len, kv_heads, group, head_dim)
    cotan_g = cotan_seq.reshape(seq_len, kv_heads, group, head_dim)
    scores = (
        jnp.einsum("ikgd,jkd->kgij", query_g, key_seq, preferred_element_type=jnp.float32) * scale
    )
    row_pos = jnp.arange(seq_len)[:, None]
    col_pos = jnp.arange(seq_len)[None, :]
    allowed = (col_pos <= row_pos) & (col_pos < length_seq)
    scores = jnp.where(allowed, scores, -1e30)
    highest = jnp.max(scores, axis=-1, keepdims=True)
    expd = jnp.where(allowed, jnp.exp(scores - highest), 0.0)
    probs = expd / jnp.sum(expd, axis=-1, keepdims=True)
    probs_low = probs.astype(jnp.bfloat16)
    value_grad = jnp.einsum(
        "kgij,ikgd->jkd", probs_low, cotan_g, preferred_element_type=jnp.float32
    ).astype(jnp.bfloat16)
    prob_grad = jnp.einsum("ikgd,jkd->kgij", cotan_g, value_seq, preferred_element_type=jnp.float32)
    centre = jnp.sum(probs * prob_grad, axis=-1, keepdims=True)
    score_grad = (probs * (prob_grad - centre) * scale).astype(jnp.bfloat16)
    rotated_grad = jnp.einsum(
        "kgij,ikgd->jkd", score_grad, query_g, preferred_element_type=jnp.float32
    )
    key_grad = rotated_grad * cosine[:, None, :] + rotate_back(rotated_grad * sine[:, None, :])
    return (key_grad.astype(jnp.bfloat16), value_grad)


def norm_backward(normed_grad, gain_f, nhat, inv_rms):
    gain_grad_in = normed_grad * gain_f
    centre = jnp.mean(gain_grad_in * nhat, axis=-1, keepdims=True)
    return ((gain_grad_in - nhat * centre) * inv_rms).astype(jnp.bfloat16)


def on_device(
    hidden_states,
    norm_gain,
    key_weight,
    value_weight,
    queries,
    context_cotangent,
    lengths,
    policy_logp,
    reference_logp,
):
    key_full, value_full = (
        lax.all_gather(key_weight[0], "dp", axis=0, tiled=True),
        lax.all_gather(value_weight[0], "dp", axis=0, tiled=True),
    )
    hidden = hidden_states[0]
    gain_f = norm_gain[0].astype(jnp.float32)
    tok_rows = hidden.shape[0]
    seq_count = lengths.shape[1]
    seq_len = tok_rows // seq_count
    kv_cols = key_full.shape[1]
    kv_local = kv_cols // HD
    q_local = queries.shape[2] // HD
    hidden_f = hidden.astype(jnp.float32)
    inv_rms = lax.rsqrt(jnp.mean(hidden_f * hidden_f, axis=-1, keepdims=True) + norm_eps)
    nhat = hidden_f * inv_rms
    normed = (nhat * gain_f).astype(jnp.bfloat16)
    key_raw = jnp.dot(normed, key_full, preferred_element_type=jnp.float32)
    values = jnp.dot(normed, value_full, preferred_element_type=jnp.float32).astype(jnp.bfloat16)
    cosine, sine = rope_tables(seq_len, HD)
    key_four = key_raw.reshape(seq_count, seq_len, kv_local, HD)
    keys = (
        key_four * cosine[None, :, None, :] + rotate_half(key_four) * sine[None, :, None, :]
    ).astype(jnp.bfloat16)
    total_seqs = seq_count * lax.axis_size("dp")
    seq_weight = 2.0 * jax.nn.sigmoid(npo_beta * (policy_logp[0] - reference_logp[0])) / total_seqs
    live = jnp.arange(seq_len)[None, :] < lengths[0][:, None]
    factor = jnp.where(live, seq_weight[:, None], 0.0)
    scaled = (
        context_cotangent[0].reshape(seq_count, seq_len, q_local, HD).astype(jnp.float32)
        * factor[:, :, None, None]
    ).astype(jnp.bfloat16)

    def one_sequence(items):
        return sequence_grads(items[0], items[1], items[2], items[3], items[4], cosine, sine)

    key_grad, value_grad = lax.map(
        one_sequence,
        (
            queries[0].reshape(seq_count, seq_len, q_local, HD),
            keys,
            values.reshape(seq_count, seq_len, kv_local, HD),
            scaled,
            lengths[0],
        ),
    )
    key_grad = key_grad.reshape(tok_rows, kv_cols)
    value_grad = value_grad.reshape(tok_rows, kv_cols)
    combined = jnp.concatenate([key_grad, value_grad], axis=1)
    grad_total = lax.psum_scatter(
        lax.dot_general(
            normed, combined, (((0,), (0,)), ((), ())), preferred_element_type=jnp.float32
        ).astype(jnp.bfloat16),
        "dp",
        scatter_dimension=0,
        tiled=True,
    )
    part = lax.dot_general(
        key_grad, key_full, (((1,), (1,)), ((), ())), preferred_element_type=jnp.float32
    )
    part = part + lax.dot_general(
        value_grad, value_full, (((1,), (1,)), ((), ())), preferred_element_type=jnp.float32
    )
    normed_grad = lax.psum(part.astype(jnp.bfloat16), "tensor").astype(jnp.float32)
    section_cot = norm_backward(normed_grad, gain_f, nhat, inv_rms)
    lower = shifted(section_cot, "pipe", -1)
    return (grad_total[:, :kv_cols][None], grad_total[:, kv_cols:][None], lower[None])


def solution(mesh):
    in_specs = (
        P("pipe", "dp", None),
        P("pipe", None),
        P("pipe", "dp", "tensor"),
        P("pipe", "dp", "tensor"),
        P("pipe", "dp", "tensor"),
        P("pipe", "dp", "tensor"),
        P("pipe", "dp"),
        P("pipe", "dp"),
        P("pipe", "dp"),
    )
    out_specs = (P("pipe", "dp", "tensor"), P("pipe", "dp", "tensor"), P("pipe", "dp", None))
    return jax.shard_map(
        on_device, mesh=mesh, in_specs=in_specs, out_specs=out_specs, check_vma=False
    )
```

profile of v0, /device:TPU:0, one launch (start us, length us, event | category | flops | bytes accessed | tf_op | source)
XLA Modules:
  0.0 366.4 jit_solution(2905376184291214419)
XLA Ops:
  7.2 0.0 copy-start.3
  7.2 0.0 all-gather.5.cloned.1.call-start
  7.2 0.7 all-gather.5.cloned.1.call-update
  7.9 0.0 all-gather.7.cloned.1.call-start
  8.0 0.7 all-gather.7.cloned.1.call-update
  8.7 0.0 all-reduce.2.cloned.1.call-start
  10.7 0.8 mul.201
  11.5 0.3 multiply_cosine_fusion
  11.9 0.8 copy.12
  12.6 0.8 copy.16
  13.4 2.3 copy.36
  15.7 0.0 copy-done.3
  15.7 0.5 copy.33
  16.2 3.1 fusion.11
  19.3 0.1 fusion.49
  19.4 44.9 %all-gather.5.cloned.1.call-done = bf16[1,8192,256]{2,1,0:T(8,128)(2,1)} async-done(((bf16[1,512,256]{2,1,0:T(8,128)(2,1)}), bf16[1,8192,256]{2,1,0:T(8,128)(2,1)}) %all-gather.5.cloned.1.call-update) | async-done | bytes 4194320 | tf_op jit(solution)/shard_map/all_gather | solution.py:87
  64.3 5.5 %fusion.20 = f32[256,256]{0,1:T(8,128)S(1)} fusion(bf16[1,8192,256]{2,1,0:T(8,128)(2,1)} %all-gather.5.cloned.1.call-done, bf16[1,256,8192]{2,1,0:T(8,128)(2,1)} %param.9, f32[8192]{0:T(1024)S(1)} %bitcast.110, f32[256]{0:T(256)S(1)} %add_rsqrt_fusion), kind=kOutput, calls=%fused_computation.28 | convolution fusion | flops 1082130432 | bytes 8684544 | tf_op jit(solution)/shard_map/dot_general | solution.py:102
  69.9 0.8 copy.13
  70.7 0.1 copy.34
  70.9 0.8 copy.35
  71.7 0.7 negate_bitcast_fusion
  72.4 45.3 %all-gather.7.cloned.1.call-done = bf16[1,8192,256]{2,1,0:T(8,128)(2,1)} async-done(((bf16[1,512,256]{2,1,0:T(8,128)(2,1)}), bf16[1,8192,256]{2,1,0:T(8,128)(2,1)}) %all-gather.7.cloned.1.call-update) | async-done | bytes 4194320 | tf_op jit(solution)/shard_map/all_gather | solution.py:88
  117.7 5.6 %fusion.37 = bf16[256,256]{0,1:T(8,128)(2,1)S(1)} fusion(bf16[1,8192,256]{2,1,0:T(8,128)(2,1)} %all-gather.7.cloned.1.call-done, bf16[1,256,8192]{2,1,0:T(8,128)(2,1)} %param.9, f32[8192]{0:T(1024)S(1)} %bitcast.111, f32[256]{0:T(256)S(1)} %add_rsqrt_fusion), kind=kOutput, calls=%fused_computation.44 | convolution fusion | flops 1082195968 | bytes 8553472 | tf_op jit(solution)/shard_map/dot_general | solution.py:103
  123.3 0.0 copy-start.4
  123.3 2.7 fusion.40
  126.0 0.0 copy-done.4
  126.0 5.0 %fusion.61 = (f32[2,8,256]{2,1,0:T(8,128)S(1)}, f32[2,8,256,256]{2,3,1,0:T(8,128)}) fusion(pred[256,256]{0,1:T(8,128)(4,1)S(1)} %fusion.49, bf16[256,2,8,128]{0,3,2,1:T(8,128)(2,1)S(1)} %bitcast.104, f32[256,2,64]{2,0,1:T(8,128)} %bitcast.115, f32[256,2,64]{2,0,1:T(8,128)} %negate_bitcast_fusion, f32[256,2,128]{2,0,1:T(8,128)} %copy.13, ...), kind=kOutput, calls=%fused_computation.80 | convolution fusion | flops 274006272 | bytes 6111232 | tf_op jit(solution)/shard_map/while/body/eval_jaxpr/sub | solution.py:53
  131.1 3.7 %fusion.34 = bf16[2,128,256]{2,1,0:T(8,128)(2,1)} fusion(f32[256,2,8,128]{0,3,2,1:T(8,128)S(1)} %bitcast.103, f32[256]{0:T(256)S(1)} %broadcast_select_fusion, f32[2,8,256,256]{2,3,1,0:T(8,128)} %get-tuple-element.42, f32[2,8,256]{2,1,0:T(8,128)S(1)} %get-tuple-element.41), kind=kOutput, calls=%fused_computation.43 | convolution fusion | flops 271646720 | bytes 6439936 | tf_op jit(solution)/shard_map/while/body/eval_jaxpr/kgij,ikgd->jkd/dot_general | solution.py:56
  134.7 7.2 %fusion.30 = f32[2,256,128]{1,2,0:T(8,128)S(1)} fusion(bf16[256,2,8,128]{0,3,2,1:T(8,128)(2,1)S(1)} %bitcast.105, f32[2,256,256,8]{2,1,3,0:T(8,128)} %fusion.40, f32[2,8,256,256]{2,3,1,0:T(8,128)} %get-tuple-element.42, f32[2,8,256]{2,1,0:T(8,128)S(1)} %get-tuple-element.41), kind=kOutput, calls=%fused_computation.41 | convolution fusion | flops 275779840 | bytes 9715712 | tf_op jit(solution)/shard_map/while/body/eval_jaxpr/kgij,ikgd->jkd/dot_general | solution.py:62
  142.1 0.0 copy-start.2
  142.1 0.0 copy-start.5
  142.1 3.6 fusion.18
  145.8 0.0 copy-done.2
  145.8 0.0 copy-done.5
  145.8 3.6 fusion.5
  149.4 0.0 all-reduce.2.cloned.1.call-update
  149.5 0.0 reduce-scatter.2.cloned.1.call-start
  149.5 7.9 %convolution_convert_fusion = bf16[8192,512]{1,0:T(8,128)(2,1)} fusion(bf16[256,256]{0,1:T(8,128)(2,1)S(1)} %bitcast.117, bf16[256,256]{0,1:T(8,128)(2,1)S(1)} %bitcast.109, bf16[1,256,8192]{2,1,0:T(8,128)(2,1)} %param.9, f32[8192]{0:T(1024)S(1)} %bitcast.112, f32[256]{0:T(256)S(1)} %add_rsqrt_fusion), kind=kOutput, calls=%fused_computation.2 | convolution fusion | flops 2160590848 | bytes 12878848 | tf_op jit(solution)/shard_map/dot_general | solution.py:135
  157.4 0.0 reduce-scatter.2.cloned.1.call-update
  157.5 106.2 %all-reduce.2.cloned.1.call-done = bf16[256,8192]{1,0:T(8,128)(2,1)} async-done(((bf16[256,8192]{1,0:T(8,128)(2,1)}), bf16[256,8192]{1,0:T(8,128)(2,1)}) %all-reduce.2.cloned.1.call-update) | async-done | bytes 4194320 | tf_op jit(solution)/shard_map/psum | solution.py:148
  263.6 5.4 %fusion.7 = f32[256]{0:T(256)S(1)} fusion(bf16[256,8192]{1,0:T(8,128)(2,1)} %all-reduce.2.cloned.1.call-done, bf16[1,256,8192]{2,1,0:T(8,128)(2,1)} %param.9, f32[8192]{0:T(1024)S(1)} %bitcast.113, f32[256]{0:T(256)S(1)} %add_rsqrt_fusion), kind=kLoop, calls=%fused_computation.11 | loop fusion | flops 12582656 | bytes 8423424 | tf_op jit(solution)/shard_map/reduce_sum | solution.py:71
  269.0 0.5 copy-done.1
  269.6 2.3 fusion.10
  271.8 1.3 collective-permute-start
  273.1 7.9 %collective-permute-done = bf16[256,8192]{1,0:T(8,128)(2,1)} collective-permute-done((bf16[256,8192]{1,0:T(8,128)(2,1)S(1)}, bf16[256,8192]{1,0:T(8,128)(2,1)}, u32[]{:S(2)}, u32[]{:S(2)}) %collective-permute-start) | collective-permute-done | bytes 4194336 | tf_op jit(solution)/shard_map/ppermute | solution.py:16
  281.0 72.4 %reduce-scatter.2.cloned.1.call-done = bf16[512,512]{1,0:T(8,128)(2,1)} async-done(((bf16[8192,512]{1,0:T(8,128)(2,1)}), bf16[512,512]{1,0:T(8,128)(2,1)}) %reduce-scatter.2.cloned.1.call-update) | async-done | bytes 524304 | tf_op jit(solution)/shard_map/reduce_scatter | solution.py:134
  353.4 1.9 slice_bitcast_fusion
  355.3 4.6 %copy.42 = bf16[1,256,8192]{2,1,0:T(8,128)(2,1)} copy(bf16[1,256,8192]{2,1,0:T(8,128)(2,1)} %bitcast.30) | data formatting | bytes 8388608
  (14 shorter events, 0.2 us)
Async XLA Ops:
  7.2 8.5 %copy-start.3 = (bf16[1,256,2048]{2,1,0:T(8,128)(2,1)S(1)}, bf16[1,256,2048]{2,1,0:T(8,128)(2,1)}, u32[]{:S(2)}) copy-start(bf16[1,256,2048]{2,1,0:T(8,128)(2,1)} %param.14) | copy-start | bytes 3145732
  7.2 57.1 %all-gather.5.cloned.1.call-start = ((), (), s32[]{:S(2)}) async-start(), calls=%async_computation.3 | async-start | bytes 4456448 | tf_op jit(solution)/shard_map/all_gather | solution.py:87
  7.9 109.8 %all-gather.7.cloned.1.call-start = ((), (), s32[]{:S(2)}) async-start(), calls=%async_computation.4 | async-start | bytes 4456448 | tf_op jit(solution)/shard_map/all_gather | solution.py:88
  8.7 255.0 %all-reduce.2.cloned.1.call-start = ((), (), s32[]{:S(2)}) async-start(), calls=%async_computation.2 | async-start | bytes 8388608 | tf_op jit(solution)/shard_map/psum | solution.py:148
  123.3 2.7 copy-start.4
  142.1 3.7 %copy-start.2 = (bf16[1,8192,256]{2,1,0:T(8,128)(2,1)S(1)}, bf16[1,8192,256]{2,1,0:T(8,128)(2,1)}, u32[]{:S(2)}) copy-start(bf16[1,8192,256]{2,1,0:T(8,128)(2,1)} %all-gather.7.cloned.1.call-done) | copy-start | bytes 12582916
  142.1 3.7 %copy-start.5 = (bf16[2,128,256]{2,1,0:T(8,128)(2,1)S(1)}, bf16[2,128,256]{2,1,0:T(8,128)(2,1)}, u32[]{:S(2)}) copy-start(bf16[2,128,256]{2,1,0:T(8,128)(2,1)} %fusion.34) | copy-start | bytes 393220
  149.5 204.0 %reduce-scatter.2.cloned.1.call-start = ((), (), s32[]{:S(2)}) async-start(), calls=%async_computation.1 | async-start | bytes 8912896 | tf_op jit(solution)/shard_map/reduce_scatter | solution.py:134
  263.6 5.4 %copy-start = (bf16[1,256,8192]{2,1,0:T(8,128)(2,1)S(1)}, bf16[1,256,8192]{2,1,0:T(8,128)(2,1)}, u32[]{:S(2)}) copy-start(bf16[1,256,8192]{2,1,0:T(8,128)(2,1)} %param.9) | copy-start | bytes 12582916
  263.6 5.9 %copy-start.1 = (bf16[256,8192]{1,0:T(8,128)(2,1)S(1)}, bf16[256,8192]{1,0:T(8,128)(2,1)}, u32[]{:S(2)}) copy-start(bf16[256,8192]{1,0:T(8,128)(2,1)} %all-reduce.2.cloned.1.call-done) | copy-start | bytes 12582916
  271.8 9.2 %collective-permute-start = (bf16[256,8192]{1,0:T(8,128)(2,1)S(1)}, bf16[256,8192]{1,0:T(8,128)(2,1)}, u32[]{:S(2)}, u32[]{:S(2)}) collective-permute-start(bf16[256,8192]{1,0:T(8,128)(2,1)S(1)} %fusion.10), channel_id=1, source_target_pairs={{32,0},{64,32},{96,64},{33,1},{65,33},{97,65},{34,2},{66,34},{98,6... | collective-permute-start | bytes 12582920 | tf_op jit(solution)/shard_map/ppermute | solution.py:16
Sparse Core Ops, SparseCore 0:
  10.2 54.1 all-gather.4
  66.5 51.2 all-gather.6
  149.6 114.0 all-reduce.1
  267.3 86.0 reduce-scatter.1
where the time goes:
time: 367 us; the launch traced here: 366 us
  waiting for transfers between devices  278 us (76%)
  matrix products  45 us (12%)
  between operations  16 us (4%)
  local copies, waits for them, and re-layouts  13.2 us (4%)
  other arithmetic  12.8 us (3%)
    psum x1, waiting for transfers between devices, on_device(): lax.psum(part.astype(jnp.bfloat16), 'tensor').astype(jnp.float32)  106 us
    reduce_scatter x1, waiting for transfers between devices, on_device(): lax.psum_scatter(lax.dot_general(normed, combined, (((0,), (0,)), ((), ()...  72.4 us
    all_gather x1, waiting for transfers between devices, on_device(): lax.all_gather(value_weight[0], 'dp', axis=0, tiled=True)  45.3 us
    all_gather x1, waiting for transfers between devices, on_device(): lax.all_gather(key_weight[0], 'dp', axis=0, tiled=True)  44.9 us
    dot_general x1, matrix products, on_device(): lax.dot_general(normed, combined, (((0,), (0,)), ((), ())), preferred_ele...  7.92 us
    ppermute x1, waiting for transfers between devices, shifted(): lax.ppermute(value, axis, [(source, source + steps) for source in range(l...  7.89 us
  transfers between devices with their start and end apart: 5, of which 5 were waited for; matrix products, arithmetic and copies ran while one was open for 9% of the time, Pallas kernels for 0%

commit v1 on v0

--- a/solution.py
+++ b/solution.py
@@ -1,13 +1,22 @@
+import functools
 import math
 import jax
 import jax.numpy as jnp
 from jax import lax
 from jax.sharding import PartitionSpec as P
+from jax.lax import all_gather
 
 HD = 128
 npo_beta = 0.1
 norm_eps = 1e-05
 rope_base = 500000.0
+
+
+def number_matrix(local_array, axis_name):
+    return all_gather(local_array, axis_name).sum(axis=0)
+
+
+track_roads = functools.partial(number_matrix, axis_name="tensor")
 
 
 def shifted(value, axis, steps):
@@ -145,7 +154,7 @@
     part = part + lax.dot_general(
         value_grad, value_full, (((1,), (1,)), ((), ())), preferred_element_type=jnp.float32
     )
-    normed_grad = lax.psum(part.astype(jnp.bfloat16), "tensor").astype(jnp.float32)
+    normed_grad = track_roads(part.astype(jnp.bfloat16)).astype(jnp.float32)
     section_cot = norm_backward(normed_grad, gain_f, nhat, inv_rms)
     lower = shifted(section_cot, "pipe", -1)
     return (grad_total[:, :kv_cols][None], grad_total[:, kv_cols:][None], lower[None])

time: 367 us -> 359 us (0.978)
  waiting for transfers between devices: 278 us -> 261 us
  other arithmetic: 12.8 us -> 21.2 us
    psum x1 -> x0, waiting for transfers between devices: 106 us -> none  [on_device(): lax.psum(part.astype(jnp.bfloat16), 'tensor').astype(jnp.float32)]
    all_gather x0 -> x1, waiting for transfers between devices: none -> 98.3 us  [number_matrix(): return all_gather(local_array, axis_name).sum(axis=0)]
    reduce_scatter x1, waiting for transfers between devices: 72.4 us -> 63.3 us  [on_device(): lax.psum_scatter(lax.dot_general(normed, combined, (((0,), (0,)), ((), ()...]
    reduce_sum x0 -> x1, other arithmetic: none -> 8.36 us  [number_matrix(): return all_gather(local_array, axis_name).sum(axis=0)]
  transfers between devices with their start and end apart: 5 -> 5, of which waited for: 5 -> 5; matrix products, arithmetic and copies ran while one was open for 9% -> 11% of each run, Pallas kernels for 0% -> 0%
where the time goes in v1:
time: 359 us; the launch traced here: 358 us
  waiting for transfers between devices  261 us (73%)
  matrix products  45 us (13%)
  other arithmetic  21.2 us (6%)
  between operations  16 us (4%)
  local copies, waits for them, and re-layouts  13.5 us (4%)
    all_gather x1, waiting for transfers between devices, number_matrix(): return all_gather(local_array, axis_name).sum(axis=0)  98.3 us
    reduce_scatter x1, waiting for transfers between devices, on_device(): lax.psum_scatter(lax.dot_general(normed, combined, (((0,), (0,)), ((), ()...  63.3 us
    all_gather x1, waiting for transfers between devices, on_device(): lax.all_gather(value_weight[0], 'dp', axis=0, tiled=True)  45.3 us
    all_gather x1, waiting for transfers between devices, on_device(): lax.all_gather(key_weight[0], 'dp', axis=0, tiled=True)  44.9 us
    reduce_sum x1, other arithmetic, number_matrix(): return all_gather(local_array, axis_name).sum(axis=0)  8.36 us
    dot_general x1, matrix products, on_device(): lax.dot_general(normed, combined, (((0,), (0,)), ((), ())), preferred_ele...  7.92 us
    ppermute x1, waiting for transfers between devices, shifted(): lax.ppermute(value, axis, [(source, source + steps) for source in range(l...  7.89 us
    dot_general x1, matrix products, sequence_grads(): jnp.einsum('kgij,ikgd->jkd', score_grad, query_g, preferred_element_type=...  7.24 us
  transfers between devices with their start and end apart: 5, of which 5 were waited for; matrix products, arithmetic and copies ran while one was open for 11% of the time, Pallas kernels for 0%

profile of v1, /device:TPU:0, one launch (start us, length us, event | category | flops | bytes accessed | tf_op | source)
XLA Modules:
  0.0 358.1 jit_solution(18377689535517699296)
XLA Ops:
  7.2 0.0 copy-start.3
  7.2 0.0 all-gather.7.cloned.1.call-start
  7.2 0.7 all-gather.7.cloned.1.call-update
  7.9 0.0 all-gather.9.cloned.1.call-start
  8.0 0.7 all-gather.9.cloned.1.call-update
  8.7 0.0 all-gather.11.cloned.1.call-start
  10.7 0.8 mul.201
  11.5 0.3 multiply_cosine_fusion
  11.9 0.8 copy.12
  12.6 0.8 copy.16
  13.4 2.3 copy.36
  15.7 0.0 copy-done.3
  15.7 0.5 copy.33
  16.2 3.1 fusion.11
  19.3 0.1 fusion.49
  19.4 44.9 %all-gather.7.cloned.1.call-done = bf16[1,8192,256]{2,1,0:T(8,128)(2,1)} async-done(((bf16[1,512,256]{2,1,0:T(8,128)(2,1)}), bf16[1,8192,256]{2,1,0:T(8,128)(2,1)}) %all-gather.7.cloned.1.call-update) | async-done | bytes 4194320 | tf_op jit(solution)/shard_map/all_gather | solution.py:96
  64.3 5.5 %fusion.20 = f32[256,256]{0,1:T(8,128)S(1)} fusion(bf16[1,8192,256]{2,1,0:T(8,128)(2,1)} %all-gather.7.cloned.1.call-done, bf16[1,256,8192]{2,1,0:T(8,128)(2,1)} %param.9, f32[8192]{0:T(1024)S(1)} %bitcast.112, f32[256]{0:T(256)S(1)} %add_rsqrt_fusion), kind=kOutput, calls=%fused_computation.28 | convolution fusion | flops 1082130432 | bytes 8684544 | tf_op jit(solution)/shard_map/dot_general | solution.py:111
  69.9 0.8 copy.13
  70.7 0.1 copy.34
  70.9 0.8 copy.35
  71.7 0.7 negate_bitcast_fusion
  72.4 45.3 %all-gather.9.cloned.1.call-done = bf16[1,8192,256]{2,1,0:T(8,128)(2,1)} async-done(((bf16[1,512,256]{2,1,0:T(8,128)(2,1)}), bf16[1,8192,256]{2,1,0:T(8,128)(2,1)}) %all-gather.9.cloned.1.call-update) | async-done | bytes 4194320 | tf_op jit(solution)/shard_map/all_gather | solution.py:97
  117.7 5.6 %fusion.37 = bf16[256,256]{0,1:T(8,128)(2,1)S(1)} fusion(bf16[1,8192,256]{2,1,0:T(8,128)(2,1)} %all-gather.9.cloned.1.call-done, bf16[1,256,8192]{2,1,0:T(8,128)(2,1)} %param.9, f32[8192]{0:T(1024)S(1)} %bitcast.113, f32[256]{0:T(256)S(1)} %add_rsqrt_fusion), kind=kOutput, calls=%fused_computation.44 | convolution fusion | flops 1082195968 | bytes 8553472 | tf_op jit(solution)/shard_map/dot_general | solution.py:112
  123.3 0.0 copy-start.4
  123.3 2.7 fusion.40
  126.0 0.0 copy-done.4
  126.0 5.0 %fusion.61 = (f32[2,8,256]{2,1,0:T(8,128)S(1)}, f32[2,8,256,256]{2,3,1,0:T(8,128)}) fusion(pred[256,256]{0,1:T(8,128)(4,1)S(1)} %fusion.49, bf16[256,2,8,128]{0,3,2,1:T(8,128)(2,1)S(1)} %bitcast.106, f32[256,2,64]{2,0,1:T(8,128)} %bitcast.117, f32[256,2,64]{2,0,1:T(8,128)} %negate_bitcast_fusion, f32[256,2,128]{2,0,1:T(8,128)} %copy.13, ...), kind=kOutput, calls=%fused_computation.80 | convolution fusion | flops 274006272 | bytes 6111232 | tf_op jit(solution)/shard_map/while/body/eval_jaxpr/sub | solution.py:62
  131.1 3.7 %fusion.34 = bf16[2,128,256]{2,1,0:T(8,128)(2,1)} fusion(f32[256,2,8,128]{0,3,2,1:T(8,128)S(1)} %bitcast.105, f32[256]{0:T(256)S(1)} %broadcast_select_fusion, f32[2,8,256,256]{2,3,1,0:T(8,128)} %get-tuple-element.42, f32[2,8,256]{2,1,0:T(8,128)S(1)} %get-tuple-element.41), kind=kOutput, calls=%fused_computation.43 | convolution fusion | flops 271646720 | bytes 6439936 | tf_op jit(solution)/shard_map/while/body/eval_jaxpr/kgij,ikgd->jkd/dot_general | solution.py:65
  134.7 7.2 %fusion.30 = f32[2,256,128]{1,2,0:T(8,128)S(1)} fusion(bf16[256,2,8,128]{0,3,2,1:T(8,128)(2,1)S(1)} %bitcast.107, f32[2,256,256,8]{2,1,3,0:T(8,128)} %fusion.40, f32[2,8,256,256]{2,3,1,0:T(8,128)} %get-tuple-element.42, f32[2,8,256]{2,1,0:T(8,128)S(1)} %get-tuple-element.41), kind=kOutput, calls=%fused_computation.41 | convolution fusion | flops 275779840 | bytes 9715712 | tf_op jit(solution)/shard_map/while/body/eval_jaxpr/kgij,ikgd->jkd/dot_general | solution.py:71
  142.1 0.0 copy-start.5
  142.1 3.6 %fusion.18 = f32[256,8192]{1,0:T(8,128)S(1)} fusion(bf16[256,256]{0,1:T(8,128)(2,1)S(1)} %bitcast.110, bf16[1,8192,256]{2,1,0:T(8,128)(2,1)} %all-gather.7.cloned.1.call-done), kind=kOutput, calls=%fused_computation.26 | convolution fusion | flops 1073741824 | bytes 12713984 | tf_op jit(solution)/shard_map/dot_general | solution.py:151
  145.8 0.0 copy-done.2
  145.8 0.0 copy-done.5
  145.8 3.6 %fusion.5 = bf16[256,8192]{1,0:T(8,128)(2,1)} fusion(f32[256,8192]{1,0:T(8,128)S(1)} %fusion.18, bf16[256,256]{0,1:T(8,128)(2,1)S(1)} %bitcast.118, bf16[1,8192,256]{2,1,0:T(8,128)(2,1)S(1)} %copy-done.2), kind=kOutput, calls=%fused_computation.9 | convolution fusion | flops 1077936128 | bytes 16908288 | tf_op jit(solution)/shard_map/dot_general | solution.py:154
  149.4 0.0 all-gather.11.cloned.1.call-update
  149.5 0.0 reduce-scatter.2.cloned.1.call-start
  149.5 7.9 %convolution_convert_fusion = bf16[8192,512]{1,0:T(8,128)(2,1)} fusion(bf16[256,256]{0,1:T(8,128)(2,1)S(1)} %bitcast.119, bf16[256,256]{0,1:T(8,128)(2,1)S(1)} %bitcast.111, bf16[1,256,8192]{2,1,0:T(8,128)(2,1)} %param.9, f32[8192]{0:T(1024)S(1)} %bitcast.114, f32[256]{0:T(256)S(1)} %add_rsqrt_fusion), kind=kOutput, calls=%fused_computation.2 | convolution fusion | flops 2160590848 | bytes 12878848 | tf_op jit(solution)/shard_map/dot_general | solution.py:144
  157.4 0.0 reduce-scatter.2.cloned.1.call-update
  157.5 98.3 %all-gather.11.cloned.1.call-done = bf16[512,8192]{1,0:T(8,128)(2,1)} async-done(((bf16[256,8192]{1,0:T(8,128)(2,1)}), bf16[512,8192]{1,0:T(8,128)(2,1)}) %all-gather.11.cloned.1.call-update) | async-done | bytes 8388624 | tf_op jit(solution)/shard_map/all_gather | solution.py:16
  255.7 8.4 %reduce_sum.53 = bf16[256,8192]{1,0:T(8,128)(2,1)} reduce(bf16[2,256,8192]{2,1,0:T(8,128)(2,1)} %bitcast.103, bf16[]{:T(256)} %constant.53.clone.1), dimensions={0}, to_apply=%region_5.6 | reduce | flops 2097152 | bytes 12582914 | tf_op jit(solution)/shard_map/reduce_sum | solution.py:16
  264.1 5.4 %fusion.7 = f32[256]{0:T(256)S(1)} fusion(bf16[256,8192]{1,0:T(8,128)(2,1)} %reduce_sum.53, bf16[1,256,8192]{2,1,0:T(8,128)(2,1)} %param.9, f32[8192]{0:T(1024)S(1)} %bitcast.115, f32[256]{0:T(256)S(1)} %add_rsqrt_fusion), kind=kLoop, calls=%fused_computation.11 | loop fusion | flops 12582656 | bytes 8423424 | tf_op jit(solution)/shard_map/reduce_sum | solution.py:80
  269.5 0.9 copy-done.1
  270.4 2.3 fusion.10
  272.6 1.3 collective-permute-start
  273.9 7.9 %collective-permute-done = bf16[256,8192]{1,0:T(8,128)(2,1)} collective-permute-done((bf16[256,8192]{1,0:T(8,128)(2,1)S(1)}, bf16[256,8192]{1,0:T(8,128)(2,1)}, u32[]{:S(2)}, u32[]{:S(2)}) %collective-permute-start) | collective-permute-done | bytes 4194336 | tf_op jit(solution)/shard_map/ppermute | solution.py:25
  281.8 63.3 %reduce-scatter.2.cloned.1.call-done = bf16[512,512]{1,0:T(8,128)(2,1)} async-done(((bf16[8192,512]{1,0:T(8,128)(2,1)}), bf16[512,512]{1,0:T(8,128)(2,1)}) %reduce-scatter.2.cloned.1.call-update) | async-done | bytes 524304 | tf_op jit(solution)/shard_map/reduce_scatter | solution.py:143
  345.1 1.9 slice_bitcast_fusion
  347.0 4.6 %copy.41 = bf16[1,256,8192]{2,1,0:T(8,128)(2,1)} copy(bf16[1,256,8192]{2,1,0:T(8,128)(2,1)} %bitcast.31) | data formatting | bytes 8388608
  (15 shorter events, 0.2 us)
Async XLA Ops:
  7.2 8.5 %copy-start.3 = (bf16[1,256,2048]{2,1,0:T(8,128)(2,1)S(1)}, bf16[1,256,2048]{2,1,0:T(8,128)(2,1)}, u32[]{:S(2)}) copy-start(bf16[1,256,2048]{2,1,0:T(8,128)(2,1)} %param.14) | copy-start | bytes 3145732
  7.2 57.1 %all-gather.7.cloned.1.call-start = ((), (), s32[]{:S(2)}) async-start(), calls=%async_computation.2 | async-start | bytes 4456448 | tf_op jit(solution)/shard_map/all_gather | solution.py:96
  7.9 109.8 %all-gather.9.cloned.1.call-start = ((), (), s32[]{:S(2)}) async-start(), calls=%async_computation.3 | async-start | bytes 4456448 | tf_op jit(solution)/shard_map/all_gather | solution.py:97
  8.7 247.1 %all-gather.11.cloned.1.call-start = ((), (), s32[]{:S(2)}) async-start(), calls=%async_computation.4 | async-start | bytes 12582912 | tf_op jit(solution)/shard_map/all_gather | solution.py:16
  123.3 2.7 copy-start.4
  142.1 3.7 %copy-start.2 = (bf16[1,8192,256]{2,1,0:T(8,128)(2,1)S(1)}, bf16[1,8192,256]{2,1,0:T(8,128)(2,1)}, u32[]{:S(2)}) copy-start(bf16[1,8192,256]{2,1,0:T(8,128)(2,1)} %all-gather.9.cloned.1.call-done) | copy-start | bytes 12582916
  142.1 3.7 %copy-start.5 = (bf16[2,128,256]{2,1,0:T(8,128)(2,1)S(1)}, bf16[2,128,256]{2,1,0:T(8,128)(2,1)}, u32[]{:S(2)}) copy-start(bf16[2,128,256]{2,1,0:T(8,128)(2,1)} %fusion.34) | copy-start | bytes 393220
  149.5 195.7 %reduce-scatter.2.cloned.1.call-start = ((), (), s32[]{:S(2)}) async-start(), calls=%async_computation.1 | async-start | bytes 8912896 | tf_op jit(solution)/shard_map/reduce_scatter | solution.py:143
  264.1 5.4 %copy-start = (bf16[1,256,8192]{2,1,0:T(8,128)(2,1)S(1)}, bf16[1,256,8192]{2,1,0:T(8,128)(2,1)}, u32[]{:S(2)}) copy-start(bf16[1,256,8192]{2,1,0:T(8,128)(2,1)} %param.9) | copy-start | bytes 12582916
  264.1 6.3 %copy-start.1 = (bf16[256,8192]{1,0:T(8,128)(2,1)S(1)}, bf16[256,8192]{1,0:T(8,128)(2,1)}, u32[]{:S(2)}) copy-start(bf16[256,8192]{1,0:T(8,128)(2,1)} %reduce_sum.53) | copy-start | bytes 12582916
  272.6 9.2 %collective-permute-start = (bf16[256,8192]{1,0:T(8,128)(2,1)S(1)}, bf16[256,8192]{1,0:T(8,128)(2,1)}, u32[]{:S(2)}, u32[]{:S(2)}) collective-permute-start(bf16[256,8192]{1,0:T(8,128)(2,1)S(1)} %fusion.10), channel_id=1, source_target_pairs={{32,0},{64,32},{96,64},{33,1},{65,33},{97,65},{34,2},{66,34},{98,6... | collective-permute-start | bytes 12582920 | tf_op jit(solution)/shard_map/ppermute | solution.py:25
Sparse Core Ops, SparseCore 0:
  10.2 54.1 all-gather.6
  66.5 51.2 all-gather.8
  149.6 106.0 all-gather.10
  259.0 86.1 reduce-scatter.1
